TPU v7x, 32 devices: a whole 2x2x4 slice. The times are simulated.
32 devices in a mesh: groups: 2 (over y), expert: 4 (over z), dp: 4 (over x, core).
Axes of the slice: x: 2, y: 2, z: 4, core: 2. Of those that a mesh axis runs over, the one named last changes fastest.
Arguments:
- out_grad: bfloat16 [4096, 2048], P(('groups', 'expert', 'dp')), parts along dimension 0, may hold values from -0.5 to 0.5
- gate_weights: bfloat16 [4096, 8], P(('groups', 'expert', 'dp')), parts along dimension 0, may hold values from 0.049804688 to 0.5
- expert_ids: int32 [4096, 8], P(('groups', 'expert', 'dp')), parts along dimension 0, may hold values from 0 to 31, all different within a row; in each aligned block of 128 rows (0 to 127, 128 to 255, ...) at most 36 rows name the same one
- hidden: bfloat16 [32, 8, 4, 36, 768], P('expert', ('groups', 'dp')), parts along dimension 1, may hold values from -6 to 6
- down_weight: bfloat16 [32, 768, 2048], P('expert', None, 'dp'), may hold values from -0.21875 to 0.21875
Outputs:
- weight_grad: float32 [64, 768, 2048], P(('groups', 'expert'), None, 'dp'), parts along dimension 0
- gate_grad: float32 [4096, 8], P(('groups', 'expert', 'dp')), parts along dimension 0
There are 2 independent parts, one for each index of `groups`. A program takes and returns all parts, laid end to end along the dimension named above; an argument that names none is the same for every part. Nothing has to cross between parts.
Inputs may be any that keep to these rules, and one draw needn't show every extreme that they name: `expert_ids`: each token names 8 different experts; within each block of 128 tokens (one device's tokens) no expert is named by more than 36 tokens, a bound that some block reaches.
All inputs are finite; a program needn't handle non-finite values.
Results may differ from a plain program's by a relative error of at most 0.0095.
Values may be sent and summed in bfloat16 or wider, within the bound.
No kernel may reach another device: no remote copies, remote signals or barrier semaphores. Data moves between devices by JAX's collectives and lax.ppermute only.
A program may use at most 128 MiB of HBM per device.

v0:
```python
import jax
import jax.numpy as jnp
from jax import lax
from jax.sharding import PartitionSpec as P


def per_device(out_grad, gate_weights, expert_ids, hidden, down_weight):
    tok_rows = out_grad.shape[0]
    top_count = expert_ids.shape[1]
    row_width = out_grad.shape[1]
    local_count = hidden.shape[0]
    peer_count = lax.axis_size("expert")
    expert_count = local_count * peer_count
    capacity = hidden.shape[3]
    hidden_width = hidden.shape[4]
    slot_rows = peer_count * capacity
    id_flat = expert_ids.reshape(-1)
    onehot = (id_flat[:, None] == jnp.arange(expert_count, dtype=jnp.int32)[None, :]).astype(
        jnp.int32
    )
    slot_index = jnp.sum((jnp.cumsum(onehot, axis=0) - 1) * onehot, axis=1)
    dest_index = id_flat * capacity + slot_index
    pair_count = tok_rows * top_count
    source_table = (
        jnp.full((expert_count * capacity,), pair_count, jnp.int32)
        .at[dest_index]
        .set(jnp.arange(pair_count, dtype=jnp.int32))
    )
    grad_ext = jnp.concatenate([out_grad, jnp.zeros((1, row_width), out_grad.dtype)], axis=0)
    gate_ext = jnp.concatenate(
        [gate_weights.reshape(-1), jnp.zeros((1,), gate_weights.dtype)], axis=0
    )
    send_grad = grad_ext[source_table // top_count].reshape(
        peer_count, local_count * capacity, row_width
    )
    send_gate = gate_ext[source_table].reshape(peer_count, local_count * capacity)
    recv_grad, recv_gate = (
        lax.all_to_all(send_grad, "expert", split_axis=0, concat_axis=0, tiled=True),
        lax.all_to_all(send_gate, "expert", split_axis=0, concat_axis=0, tiled=True),
    )
    recv_grad = recv_grad.reshape(peer_count, local_count, capacity, row_width).transpose(
        1, 0, 2, 3
    )
    recv_grad = recv_grad.reshape(local_count, slot_rows, row_width)
    recv_gate = recv_gate.reshape(peer_count, local_count, capacity).transpose(1, 0, 2)
    recv_gate = recv_gate.reshape(local_count, slot_rows)
    scaled = (recv_gate.astype(jnp.float32)[:, :, None] * recv_grad).astype(jnp.bfloat16)
    hidden_rows = hidden.reshape(local_count, slot_rows, hidden_width)
    shards = lax.axis_size("dp")
    column_part = scaled.reshape(local_count, slot_rows, shards, row_width // shards)
    columns_in = lax.all_to_all(column_part, "dp", split_axis=2, concat_axis=2, tiled=True)
    hidden_all = lax.all_gather(hidden_rows[:, None], "dp", axis=1, tiled=True)
    partial_value = jnp.einsum(
        "eirf,erid->eifd", hidden_all, columns_in, preferred_element_type=jnp.float32
    ).astype(jnp.bfloat16)
    weight_grad = jnp.sum(partial_value.astype(jnp.float32), axis=1)
    full_weight = lax.all_gather(down_weight, "dp", axis=2, tiled=True)
    expert_out = jnp.einsum(
        "erf,efd->erd", hidden_rows, full_weight, preferred_element_type=jnp.float32
    )
    slot_grad = jnp.sum(recv_grad * expert_out, axis=2)
    send_back = slot_grad.reshape(local_count, peer_count, capacity).transpose(1, 0, 2)
    send_back = send_back.reshape(peer_count, local_count * capacity)
    returned = lax.all_to_all(send_back, "expert", split_axis=0, concat_axis=0, tiled=True)
    gate_grad = returned.reshape(-1)[dest_index].reshape(tok_rows, top_count)
    return (weight_grad, gate_grad)


def solution(mesh):
    return jax.shard_map(
        per_device,
        mesh=mesh,
        in_specs=(
            P(("groups", "expert", "dp"), None),
            P(("groups", "expert", "dp"), None),
            P(("groups", "expert", "dp"), None),
            P("expert", ("groups", "dp"), None, None, None),
            P("expert", None, "dp"),
        ),
        out_specs=(P(("groups", "expert"), None, "dp"), P(("groups", "expert", "dp"), None)),
        check_vma=False,
    )
```

profile of v0, /device:TPU:0, one launch (start us, length us, event | category | flops | bytes accessed | tf_op | source)
XLA Modules:
  0.0 316.2 jit_solution(5351354100891161966)
XLA Ops:
  7.2 0.7 all-gather.5.cloned.1.call-update
  7.9 0.8 copy.44
  8.7 0.1 eq.29
  8.8 0.1 eq.25
  8.9 9.0 %reduce-window.6 = s32[32,8,128]{2,1,0:T(8,128)S(1)} reduce-window(s32[32,8,128]{2,1,0:T(8,128)S(1)} %fusion.5, s32[]{:T(128)} %constant.16.clone.1), window={size=1x1x128 pad=0_0x0_0x127_0}, to_apply=%region_0.0 | reduce-window | flops 4161536 | bytes 262148 | tf_op jit(solution)/shard_map/reduce-window
  17.9 0.1 slice.14
  18.0 0.1 copy.46
  18.2 0.1 copy.47
  18.3 0.1 copy.43
  18.4 0.1 mul.33
  18.5 0.1 copy.42
  18.6 0.1 reshape.103
  18.7 0.1 add_add_fusion
  18.9 4.3 %scatter_custom_fusion = s32[1152]{0:T(1024)S(1)} fusion(s32[1024]{0:T(1024)S(1)} %bitcast.43, s32[1024]{0:T(1024)S(1)} %iota.11, s32[]{:T(128)} %constant.12.clone.1), kind=kCustom, calls=%fused_computation.31 | custom fusion | bytes 4612 | tf_op jit(solution)/shard_map/scatter | solution.py:27
  23.3 7.3 %gather_fusion = bf16[1152]{0:T(1024)(128)(2,1)S(1)} fusion(bf16[1025]{0:T(1024)(128)(2,1)S(1)} %pad_maximum_fusion, s32[2048]{0:T(1024)S(1)} %get-tuple-element.11), kind=kCustom, calls=%fused_computation | custom fusion | bytes 9216 | tf_op jit(solution)/shard_map/gather | solution.py:36
  30.6 0.1 all_to_all.24
  30.7 0.5 broadcast.92
  31.2 0.7 reduce.4
  31.8 0.7 reshape.154
  32.5 6.3 %all-to-all-start = ((bf16[4,2,144]{2,1,0:T(2,128)(2,1)}), bf16[4,2,144]{2,1,0:T(2,128)(2,1)S(1)}, u32[]{:S(2)}, u32[]{:S(2)}) async-start(bf16[4,2,144]{2,1,0:T(2,128)(2,1)} %reshape.154), calls=%async_computation | async-start | bytes 8192 | tf_op jit(solution)/shard_map/all_to_all | solution.py:39
  38.9 5.9 %gather_fusion.1 = bf16[1152,2048]{1,0:T(8,128)(2,1)} fusion(bf16[129,2048]{1,0:T(8,128)(2,1)S(1)} %concatenate.7, s32[2048]{0:T(1024)S(1)} %get-tuple-element.10), kind=kCustom, calls=%fused_computation.1 | custom fusion | bytes 9441792 | tf_op jit(solution)/shard_map/gather | solution.py:33
  44.8 5.2 %all-to-all-start.1 = ((bf16[4,288,2048]{2,1,0:T(8,128)(2,1)}), bf16[4,288,2048]{2,1,0:T(8,128)(2,1)}, u32[]{:S(2)}, u32[]{:S(2)}) async-start(bf16[4,288,2048]{2,1,0:T(8,128)(2,1)} %bitcast.34), calls=%async_computation.1 | async-start | bytes 9437184 | tf_op jit(solution)/shard_map/all_to_all | solution.py:38
  50.0 0.2 all-gather.3.cloned.1.call-start
  50.2 0.5 copy.54
  50.8 1.2 copy-done
  52.0 1.6 copy.55
  53.5 0.1 reshape.155
  53.7 0.1 reshape.113
  53.8 0.1 reshape.110
  53.8 0.1 copy.50
  53.9 100.5 %all-to-all-done.1 = bf16[4,288,2048]{2,1,0:T(8,128)(2,1)} async-done(((bf16[4,288,2048]{2,1,0:T(8,128)(2,1)}), bf16[4,288,2048]{2,1,0:T(8,128)(2,1)}, u32[]{:S(2)}, u32[]{:S(2)}) %all-to-all-start.1) | async-done | bytes 4718624 | tf_op jit(solution)/shard_map/all_to_all | solution.py:38
  154.4 6.0 %copy.51 = f32[4,288,2048]{2,0,1:T(4,128)S(1)} copy(bf16[4,288,2048]{2,1,0:T(8,128)(2,1)} %all-to-all-done.1) | data formatting | bytes 14155776 | tf_op jit(solution)/shard_map/convert_element_type | solution.py:47
  160.4 9.2 %copy.52 = f32[8,4,36,2048]{3,0,2,1:T(8,128)} copy(f32[8,4,36,2048]{3,1,2,0:T(4,128)S(1)} %bitcast.33) | data formatting | bytes 18874368 | tf_op jit(solution)/shard_map/convert_element_type | solution.py:47
  169.6 12.6 %reshape.111 = f32[8,144,4,512]{3,2,0,1:T(4,128)} reshape(f32[8,4,36,2048]{3,0,2,1:T(8,128)} %copy.52) | data formatting | bytes 18874368 | tf_op jit(solution)/shard_map/convert_element_type | solution.py:47
  182.2 6.1 %multiply_convert_fusion = bf16[8,144,4,512]{3,2,0,1:T(4,128)(2,1)S(1)} fusion(f32[8,144,4,512]{3,2,0,1:T(4,128)} %reshape.111, f32[8,144]{0,1:T(8,128)S(1)} %copy.50), kind=kLoop, calls=%fused_computation.7 | loop fusion | flops 4718592 | bytes 14160384 | tf_op jit(solution)/shard_map/convert_element_type | solution.py:47
  188.2 4.8 %copy.53 = bf16[8,144,4,512]{3,1,0,2:T(8,128)(2,1)} copy(bf16[8,144,4,512]{3,2,0,1:T(4,128)(2,1)S(1)} %multiply_convert_fusion) | data formatting | bytes 9437184 | tf_op jit(solution)/shard_map/convert_element_type | solution.py:47
  193.0 5.2 %all-to-all-start.2 = ((bf16[8,144,4,512]{3,1,0,2:T(8,128)(2,1)}), bf16[8,144,4,512]{3,1,0,2:T(8,128)(2,1)}, u32[]{:S(2)}, u32[]{:S(2)}) async-start(bf16[8,144,4,512]{3,1,0,2:T(8,128)(2,1)} %copy.53), calls=%async_computation.2 | async-start | bytes 9437184 | tf_op jit(solution)/shard_map/all_to_all | solution.py:51
  198.3 20.2 %fusion = f32[8,144]{1,0:T(8,128)S(1)} fusion(f32[8,144,2048]{2,0,1:T(8,128)} %bitcast.32, bf16[8,768,2048]{2,1,0:T(8,128)(2,1)} %all-gather.5.cloned.1.call-done, bf16[8,144,768]{2,0,1:T(8,128)(2,1)S(1)} %bitcast.36), kind=kOutput, calls=%fused_computation.6 | convolution fusion | flops 3628596224 | bytes 36377088 | tf_op jit(solution)/shard_map/erf,efd->erd/dot_general | solution.py:58
  218.5 0.1 reshape.107
  218.6 0.7 all_to_all.25
  219.3 49.3 %all-to-all-done.2 = bf16[8,144,4,512]{3,1,0,2:T(8,128)(2,1)} async-done(((bf16[8,144,4,512]{3,1,0,2:T(8,128)(2,1)}), bf16[8,144,4,512]{3,1,0,2:T(8,128)(2,1)}, u32[]{:S(2)}, u32[]{:S(2)}) %all-to-all-start.2) | async-done | bytes 4718624 | tf_op jit(solution)/shard_map/all_to_all | solution.py:51
  268.6 4.6 %all-to-all-start.3 = ((f32[4,1,288]{2,1,0:T(1,128)}), f32[4,1,288]{2,1,0:T(1,128)S(1)}, u32[]{:S(2)}, u32[]{:S(2)}) async-start(f32[4,1,288]{2,1,0:T(1,128)} %all_to_all.25), calls=%async_computation.3 | async-start | bytes 12288 | tf_op jit(solution)/shard_map/all_to_all | solution.py:64
  273.2 16.6 %convert_reduce_fusion = f32[8,512,768]{2,1,0:T(8,128)} fusion(bf16[8,4,144,768]{3,2,1,0:T(8,128)(2,1)} %all-gather.3.cloned.1.call-done, bf16[8,144,4,512]{3,1,0,2:T(8,128)(2,1)} %all-to-all-done.2), kind=kOutput, calls=%fused_computation.4 | convolution fusion | flops 3658481664 | bytes 24379392 | tf_op jit(solution)/shard_map/eirf,erid->eifd/dot_general | solution.py:53
  289.7 12.6 %copy.63 = f32[8,768,512]{2,1,0:T(8,128)} copy(f32[8,768,512]{1,2,0:T(8,128)} %bitcast.37) | data formatting | bytes 25165824
  302.4 0.1 reshape.108
  302.4 6.2 %gather_fusion.2 = f32[1024]{0:T(1024)S(1)} fusion(f32[1152]{0:T(1024)S(1)} %reshape.108, s32[1024]{0:T(1024)S(1)} %broadcast_clamp_fusion), kind=kCustom, calls=%fused_computation.2 | custom fusion | bytes 12288 | tf_op jit(solution)/shard_map/gather | solution.py:65
  308.6 0.1 reshape.109
  308.7 0.7 copy.64
  (33 shorter events, 0.3 us)
Async XLA Ops:
  7.2 11.1 %copy-start.4 = (s32[128,8]{0,1:T(8,128)S(1)}, s32[128,8]{0,1:T(8,128)}, u32[]{:S(2)}) copy-start(s32[128,8]{0,1:T(8,128)} %param.7) | copy-start | bytes 12292
  7.2 11.3 %copy-start.5 = (bf16[128,8]{0,1:T(8,128)(2,1)S(1)}, bf16[128,8]{0,1:T(8,128)(2,1)}, u32[]{:S(2)}) copy-start(bf16[128,8]{0,1:T(8,128)(2,1)} %param.6) | copy-start | bytes 6148
  7.2 31.7 %copy-start.3 = (bf16[128,2048]{1,0:T(8,128)(2,1)S(1)}, bf16[128,2048]{1,0:T(8,128)(2,1)}, u32[]{:S(2)}) copy-start(bf16[128,2048]{1,0:T(8,128)(2,1)} %param.5) | copy-start | bytes 1572868
  7.2 191.1 %all-gather.5.cloned.1.call-start = ((), (), s32[]{:S(2)}) async-start(), calls=%async_computation.5 | async-start | bytes 31457280 | tf_op jit(solution)/shard_map/all_gather | solution.py:57
  32.5 12.3 %all-to-all-start = ((bf16[4,2,144]{2,1,0:T(2,128)(2,1)}), bf16[4,2,144]{2,1,0:T(2,128)(2,1)S(1)}, u32[]{:S(2)}, u32[]{:S(2)}) async-start(bf16[4,2,144]{2,1,0:T(2,128)(2,1)} %reshape.154), calls=%async_computation | async-start | bytes 8192 | tf_op jit(solution)/shard_map/all_to_all | solution.py:39
  44.8 5.4 %copy-start.2 = (bf16[8,1,4,36,768]{4,2,3,1,0:T(4,128)(2,1)S(1)}, bf16[8,1,4,36,768]{4,2,3,1,0:T(4,128)(2,1)}, u32[]{:S(2)}) copy-start(bf16[8,1,4,36,768]{4,2,3,1,0:T(4,128)(2,1)} %param.8) | copy-start | bytes 5308420
  44.8 109.6 %all-to-all-start.1 = ((bf16[4,288,2048]{2,1,0:T(8,128)(2,1)}), bf16[4,288,2048]{2,1,0:T(8,128)(2,1)}, u32[]{:S(2)}, u32[]{:S(2)}) async-start(bf16[4,288,2048]{2,1,0:T(8,128)(2,1)} %bitcast.34), calls=%async_computation.1 | async-start | bytes 9437184 | tf_op jit(solution)/shard_map/all_to_all | solution.py:38
  50.0 223.1 %all-gather.3.cloned.1.call-start = ((), (), s32[]{:S(2)}) async-start(), calls=%async_computation.4 | async-start | bytes 8847360 | tf_op jit(solution)/shard_map/all_gather | solution.py:52
  50.8 1.2 copy-start
  193.0 5.2 %copy-start.1 = (bf16[8,1,4,36,768]{4,0,3,2,1:T(8,128)(2,1)S(1)}, bf16[8,1,4,36,768]{4,0,3,2,1:T(8,128)(2,1)}, u32[]{:S(2)}) copy-start(bf16[8,1,4,36,768]{4,0,3,2,1:T(8,128)(2,1)} %copy-done) | copy-start | bytes 5308420
  193.0 75.5 %all-to-all-start.2 = ((bf16[8,144,4,512]{3,1,0,2:T(8,128)(2,1)}), bf16[8,144,4,512]{3,1,0,2:T(8,128)(2,1)}, u32[]{:S(2)}, u32[]{:S(2)}) async-start(bf16[8,144,4,512]{3,1,0,2:T(8,128)(2,1)} %copy.53), calls=%async_computation.2 | async-start | bytes 9437184 | tf_op jit(solution)/shard_map/all_to_all | solution.py:51
  268.6 33.8 %all-to-all-start.3 = ((f32[4,1,288]{2,1,0:T(1,128)}), f32[4,1,288]{2,1,0:T(1,128)S(1)}, u32[]{:S(2)}, u32[]{:S(2)}) async-start(f32[4,1,288]{2,1,0:T(1,128)} %all_to_all.25), calls=%async_computation.3 | async-start | bytes 12288 | tf_op jit(solution)/shard_map/all_to_all | solution.py:64
Sparse Core Ops, SparseCore 0:
  9.6 157.5 all-gather.4
  168.7 67.3 all-gather.2
where the time goes:
time: 317 us; the launch traced here: 316 us
  waiting for transfers between devices  150 us (47%)
  local copies, waits for them, and re-layouts  77.1 us (24%)
  matrix products  36.8 us (12%)
  starting transfers between devices  21.5 us (7%)
  other arithmetic  16 us (5%)
  between operations  14.3 us (5%)
    all_to_all x1, waiting for transfers between devices, per_device(): lax.all_to_all(send_grad, 'expert', split_axis=0, concat_axis=0, tiled=True)  100 us
    all_to_all x1, waiting for transfers between devices, per_device(): lax.all_to_all(column_part, 'dp', split_axis=2, concat_axis=2, tiled=True)  49.3 us
    convert_element_type x7, local copies, waits for them, and re-layouts, per_device(): recv_gate.astype(jnp.float32)[:, :, None] * recv_grad  28 us
    dot_general x1, matrix products, per_device(): jnp.einsum('erf,efd->erd', hidden_rows, full_weight, preferred_element_ty...  20.2 us
    unnamed x19, local copies, waits for them, and re-layouts  16.7 us
    dot_general x1, matrix products, per_device(): jnp.einsum('eirf,erid->eifd', hidden_all, columns_in, preferred_element_t...  16.6 us
    another operation x2, other arithmetic  9.04 us
    gather x1, local copies, waits for them, and re-layouts, per_device(): gate_ext[source_table].reshape(peer_count, local_count * capacity)  7.27 us
  transfers between devices with their start and end apart: 6, of which 2 were waited for; matrix products, arithmetic and copies ran while one was open for 38% of the time, Pallas kernels for 0%

commit v1 on v0

--- a/solution.py
+++ b/solution.py
@@ -2,9 +2,17 @@
 import jax.numpy as jnp
 from jax import lax
 from jax.sharding import PartitionSpec as P
+from jax.lax import all_to_all, axis_size
 
 
 def per_device(out_grad, gate_weights, expert_ids, hidden, down_weight):
+
+    def _load_strips_all(local_x, which_dim, k_dim):
+        return jnp.concatenate(
+            all_to_all(jnp.stack(jnp.split(local_x, axis_size("dp"), axis=which_dim)), "dp", 0, 0),
+            axis=k_dim,
+        )
+
     tok_rows = out_grad.shape[0]
     top_count = expert_ids.shape[1]
     row_width = out_grad.shape[1]
@@ -48,7 +56,7 @@
     hidden_rows = hidden.reshape(local_count, slot_rows, hidden_width)
     shards = lax.axis_size("dp")
     column_part = scaled.reshape(local_count, slot_rows, shards, row_width // shards)
-    columns_in = lax.all_to_all(column_part, "dp", split_axis=2, concat_axis=2, tiled=True)
+    columns_in = _load_strips_all(column_part, 2, k_dim=2)
     hidden_all = lax.all_gather(hidden_rows[:, None], "dp", axis=1, tiled=True)
     partial_value = jnp.einsum(
         "eirf,erid->eifd", hidden_all, columns_in, preferred_element_type=jnp.float32

time: 317 us -> 321 us (1.013); the launches traced: 316 us -> 317 us
  waiting for transfers between devices: 150 us -> 137 us
  local copies, waits for them, and re-layouts: 77.1 us -> 87.9 us
    split x0 -> x5, local copies, waits for them, and re-layouts: none -> 15.7 us  [_load_strips_all(): jnp.split(local_x, axis_size('dp'), axis=which_dim)]
    all_to_all x1, waiting for transfers between devices: 49.3 us -> 35.8 us  [_load_strips_all(): all_to_all(jnp.stack(jnp.split(local_x, axis_size('dp'), axis=which_dim))...]
    convert_element_type x1 -> x0, local copies, waits for them, and re-layouts: 4.8 us -> none  [per_device(): (recv_gate.astype(jnp.float32)[:, :, None] * recv_grad).astype(jnp.bfloat16)]
    another operation x2 -> x3, other arithmetic: 9.04 us -> 11.5 us
  transfers between devices with their start and end apart: 6 -> 6, of which waited for: 2 -> 2; matrix products, arithmetic and copies ran while one was open for 38% -> 42% of each run, Pallas kernels for 0% -> 0%
where the time goes in v1:
time: 321 us; the launch traced here: 317 us
  waiting for transfers between devices  137 us (43%)
  local copies, waits for them, and re-layouts  87.9 us (27%)
  matrix products  36.8 us (11%)
  starting transfers between devices  22 us (7%)
  other arithmetic  18.5 us (6%)
  between operations  14.6 us (5%)
    all_to_all x1, waiting for transfers between devices, per_device(): lax.all_to_all(send_grad, 'expert', split_axis=0, concat_axis=0, tiled=True)  100 us
    all_to_all x1, waiting for transfers between devices, _load_strips_all(): all_to_all(jnp.stack(jnp.split(local_x, axis_size('dp'), axis=which_dim))...  35.8 us
    convert_element_type x7, local copies, waits for them, and re-layouts, per_device(): recv_gate.astype(jnp.float32)[:, :, None] * recv_grad  28.6 us
    dot_general x1, matrix products, per_device(): jnp.einsum('erf,efd->erd', hidden_rows, full_weight, preferred_element_ty...  20.2 us
    dot_general x1, matrix products, per_device(): jnp.einsum('eirf,erid->eifd', hidden_all, columns_in, preferred_element_t...  16.6 us
    unnamed x19, local copies, waits for them, and re-layouts  16 us
    split x5, local copies, waits for them, and re-layouts, _load_strips_all(): jnp.split(local_x, axis_size('dp'), axis=which_dim)  15.7 us
    another operation x2, other arithmetic  9.04 us
  transfers between devices with their start and end apart: 6, of which 2 were waited for; matrix products, arithmetic and copies ran while one was open for 42% of the time, Pallas kernels for 0%

profile of v1, /device:TPU:0, one launch (start us, length us, event | category | flops | bytes accessed | tf_op | source)
XLA Modules:
  0.0 316.7 jit_solution(3216414738815729904)
XLA Ops:
  7.2 0.7 all-gather.5.cloned.1.call-update
  7.9 0.1 copy.163
  8.0 0.1 eq.29
  8.1 0.1 eq.25
  8.2 9.0 %reduce-window.6 = s32[32,8,128]{2,1,0:T(8,128)S(1)} reduce-window(s32[32,8,128]{2,1,0:T(8,128)S(1)} %fusion.6, s32[]{:T(128)} %constant.16.clone.1), window={size=1x1x128 pad=0_0x0_0x127_0}, to_apply=%region_0.0 | reduce-window | flops 4161536 | bytes 262148 | tf_op jit(solution)/shard_map/reduce-window
  17.3 0.1 slice.14
  17.4 0.1 copy.165
  17.6 0.1 copy.162
  17.7 0.1 mul.33
  17.8 0.1 copy.161
  17.9 0.1 reshape.109
  18.1 0.1 add_add_fusion
  18.2 4.3 %scatter_custom_fusion = s32[1152]{0:T(1024)S(1)} fusion(s32[1024]{0:T(1024)S(1)} %bitcast.64, s32[1024]{0:T(1024)S(1)} %iota.11, s32[]{:T(128)} %constant.12.clone.1), kind=kCustom, calls=%fused_computation.37 | custom fusion | bytes 4612 | tf_op jit(solution)/shard_map/scatter | solution.py:35
  22.6 7.3 %gather_fusion = bf16[1152]{0:T(1024)(128)(2,1)S(1)} fusion(bf16[1025]{0:T(1024)(128)(2,1)S(1)} %pad_maximum_fusion.1, s32[2048]{0:T(1024)S(1)} %get-tuple-element.23), kind=kCustom, calls=%fused_computation | custom fusion | bytes 9216 | tf_op jit(solution)/shard_map/gather | solution.py:44
  29.9 0.1 all_to_all.24
  30.0 0.5 broadcast.92
  30.5 0.7 reduce.4
  31.2 0.7 reshape.162
  31.8 6.3 %all-to-all-start = ((bf16[4,2,144]{2,1,0:T(2,128)(2,1)}), bf16[4,2,144]{2,1,0:T(2,128)(2,1)S(1)}, u32[]{:S(2)}, u32[]{:S(2)}) async-start(bf16[4,2,144]{2,1,0:T(2,128)(2,1)} %reshape.162), calls=%async_computation | async-start | bytes 8192 | tf_op jit(solution)/shard_map/all_to_all | solution.py:47
  38.2 5.9 %gather_fusion.1 = bf16[1152,2048]{1,0:T(8,128)(2,1)} fusion(bf16[129,2048]{1,0:T(8,128)(2,1)S(1)} %concatenate.7, s32[2048]{0:T(1024)S(1)} %get-tuple-element.22), kind=kCustom, calls=%fused_computation.1 | custom fusion | bytes 9441792 | tf_op jit(solution)/shard_map/gather | solution.py:41
  44.1 5.2 %all-to-all-start.1 = ((bf16[4,288,2048]{2,1,0:T(8,128)(2,1)}), bf16[4,288,2048]{2,1,0:T(8,128)(2,1)}, u32[]{:S(2)}, u32[]{:S(2)}) async-start(bf16[4,288,2048]{2,1,0:T(8,128)(2,1)} %bitcast.51), calls=%async_computation.1 | async-start | bytes 9437184 | tf_op jit(solution)/shard_map/all_to_all | solution.py:46
  49.4 0.3 all-gather.3.cloned.1.call-start
  49.7 0.5 copy.177
  50.2 1.2 copy-done
  51.4 1.6 copy.178
  53.0 0.1 reshape.163
  53.3 0.1 copy.169
  53.4 100.3 %all-to-all-done.1 = bf16[4,288,2048]{2,1,0:T(8,128)(2,1)} async-done(((bf16[4,288,2048]{2,1,0:T(8,128)(2,1)}), bf16[4,288,2048]{2,1,0:T(8,128)(2,1)}, u32[]{:S(2)}, u32[]{:S(2)}) %all-to-all-start.1) | async-done | bytes 4718624 | tf_op jit(solution)/shard_map/all_to_all | solution.py:46
  153.7 6.0 %copy.170 = f32[4,288,2048]{2,0,1:T(4,128)S(1)} copy(bf16[4,288,2048]{2,1,0:T(8,128)(2,1)} %all-to-all-done.1) | data formatting | bytes 14155776 | tf_op jit(solution)/shard_map/convert_element_type | solution.py:55
  159.7 9.2 %copy.171 = f32[8,4,36,2048]{3,0,2,1:T(8,128)} copy(f32[8,4,36,2048]{3,1,2,0:T(4,128)S(1)} %bitcast.50) | data formatting | bytes 18874368 | tf_op jit(solution)/shard_map/convert_element_type | solution.py:55
  168.9 13.2 %reshape.119 = f32[8,144,4,512]{3,2,0,1:T(4,128)} reshape(f32[8,4,36,2048]{3,0,2,1:T(8,128)} %copy.171) | data formatting | bytes 18874368 | tf_op jit(solution)/shard_map/convert_element_type | solution.py:55
  182.1 6.1 %multiply_convert_fusion = bf16[8,144,4,512]{3,2,0,1:T(4,128)(2,1)S(1)} fusion(f32[8,144,4,512]{3,2,0,1:T(4,128)} %reshape.119, f32[8,144]{0,1:T(8,128)S(1)} %copy.169), kind=kLoop, calls=%fused_computation.7 | loop fusion | flops 4718592 | bytes 14160384 | tf_op jit(solution)/shard_map/convert_element_type | solution.py:55
  188.2 10.7 %fusion.11 = (bf16[8,144,1,512]{3,2,0,1:T(2,128)(2,1)S(1)}, bf16[8,144,1,512]{3,2,0,1:T(2,128)(2,1)S(1)}, bf16[8,144,1,512]{3,2,0,1:T(2,128)(2,1)S(1)}, bf16[8,144,1,512]{3,2,0,1:T(2,128)(2,1)S(1)}) fusion(bf16[8,144,4,512]{3,2,0,1:T(4,128)(2,1)S(1)} %multiply_convert_fusion), kind=kLoop, calls=%fused_computation.41 | loop fusion | bytes 9437184 | tf_op jit(solution)/shard_map/split | solution.py:12
  198.8 1.3 copy.202
  200.1 1.3 copy.203
  201.4 1.3 copy.204
  202.6 1.3 copy.205
  203.9 2.5 pad_maximum_fusion
  206.3 5.3 %all-to-all-start.2 = ((bf16[4,8,144,1,512]{4,2,1,3,0:T(8,128)(2,1)}), bf16[4,8,144,1,512]{4,2,1,3,0:T(8,128)(2,1)}, u32[]{:S(2)}, u32[]{:S(2)}) async-start(bf16[4,8,144,1,512]{4,2,1,3,0:T(8,128)(2,1)} %pad_maximum_fusion), calls=%async_computation.2 | async-start | bytes 9437184 | tf_op jit(solution)/shard_map/all_to_all | solution.py:12
  211.7 20.2 %fusion = f32[8,144]{1,0:T(8,128)S(1)} fusion(f32[8,144,2048]{2,0,1:T(8,128)} %bitcast.49, bf16[8,768,2048]{2,1,0:T(8,128)(2,1)} %all-gather.5.cloned.1.call-done, bf16[8,144,768]{2,0,1:T(8,128)(2,1)S(1)} %bitcast.53), kind=kOutput, calls=%fused_computation.6 | convolution fusion | flops 3628596224 | bytes 36377088 | tf_op jit(solution)/shard_map/erf,efd->erd/dot_general | solution.py:66
  232.1 0.7 all_to_all.25
  232.8 35.8 %all-to-all-done.2 = bf16[4,8,144,1,512]{4,2,1,3,0:T(8,128)(2,1)} async-done(((bf16[4,8,144,1,512]{4,2,1,3,0:T(8,128)(2,1)}), bf16[4,8,144,1,512]{4,2,1,3,0:T(8,128)(2,1)}, u32[]{:S(2)}, u32[]{:S(2)}) %all-to-all-start.2) | async-done | bytes 4718624 | tf_op jit(solution)/shard_map/all_to_all | solution.py:12
  268.5 4.8 %all-to-all-start.3 = ((f32[4,1,288]{2,1,0:T(1,128)}), f32[4,1,288]{2,1,0:T(1,128)S(1)}, u32[]{:S(2)}, u32[]{:S(2)}) async-start(f32[4,1,288]{2,1,0:T(1,128)} %all_to_all.25), calls=%async_computation.3 | async-start | bytes 12288 | tf_op jit(solution)/shard_map/all_to_all | solution.py:72
  273.4 16.6 %convert_reduce_fusion = f32[8,512,768]{2,1,0:T(8,128)} fusion(bf16[8,4,144,768]{3,2,1,0:T(8,128)(2,1)} %all-gather.3.cloned.1.call-done, bf16[4,8,144,1,512]{4,2,1,3,0:T(8,128)(2,1)} %all-to-all-done.2), kind=kOutput, calls=%fused_computation.4 | convolution fusion | flops 3658481664 | bytes 24379392 | tf_op jit(solution)/shard_map/eirf,erid->eifd/dot_general | solution.py:61
  290.0 12.6 %copy.185 = f32[8,768,512]{2,1,0:T(8,128)} copy(f32[8,768,512]{1,2,0:T(8,128)} %bitcast.54) | data formatting | bytes 25165824
  302.7 6.2 %gather_fusion.2 = f32[1024]{0:T(1024)S(1)} fusion(f32[1152]{0:T(1024)S(1)} %reshape.116, s32[1024]{0:T(1024)S(1)} %broadcast_clamp_fusion), kind=kCustom, calls=%fused_computation.2 | custom fusion | bytes 12288 | tf_op jit(solution)/shard_map/gather | solution.py:73
  308.8 0.1 reshape.117
  308.9 0.7 copy.186
  (38 shorter events, 0.8 us)
Async XLA Ops:
  7.2 0.8 copy-start.4
  7.2 10.6 %copy-start.5 = (bf16[128,8]{0,1:T(8,128)(2,1)S(1)}, bf16[128,8]{0,1:T(8,128)(2,1)}, u32[]{:S(2)}) copy-start(bf16[128,8]{0,1:T(8,128)(2,1)} %param.6) | copy-start | bytes 6148
  7.2 31.0 %copy-start.3 = (bf16[128,2048]{1,0:T(8,128)(2,1)S(1)}, bf16[128,2048]{1,0:T(8,128)(2,1)}, u32[]{:S(2)}) copy-start(bf16[128,2048]{1,0:T(8,128)(2,1)} %param.5) | copy-start | bytes 1572868
  7.2 204.5 %all-gather.5.cloned.1.call-start = ((), (), s32[]{:S(2)}) async-start(), calls=%async_computation.5 | async-start | bytes 31457280 | tf_op jit(solution)/shard_map/all_gather | solution.py:65
  31.8 12.3 %all-to-all-start = ((bf16[4,2,144]{2,1,0:T(2,128)(2,1)}), bf16[4,2,144]{2,1,0:T(2,128)(2,1)S(1)}, u32[]{:S(2)}, u32[]{:S(2)}) async-start(bf16[4,2,144]{2,1,0:T(2,128)(2,1)} %reshape.162), calls=%async_computation | async-start | bytes 8192 | tf_op jit(solution)/shard_map/all_to_all | solution.py:47
  44.1 5.5 %copy-start.2 = (bf16[8,1,4,36,768]{4,2,3,1,0:T(4,128)(2,1)S(1)}, bf16[8,1,4,36,768]{4,2,3,1,0:T(4,128)(2,1)}, u32[]{:S(2)}) copy-start(bf16[8,1,4,36,768]{4,2,3,1,0:T(4,128)(2,1)} %param.8) | copy-start | bytes 5308420
  44.1 109.6 %all-to-all-start.1 = ((bf16[4,288,2048]{2,1,0:T(8,128)(2,1)}), bf16[4,288,2048]{2,1,0:T(8,128)(2,1)}, u32[]{:S(2)}, u32[]{:S(2)}) async-start(bf16[4,288,2048]{2,1,0:T(8,128)(2,1)} %bitcast.51), calls=%async_computation.1 | async-start | bytes 9437184 | tf_op jit(solution)/shard_map/all_to_all | solution.py:46
  49.4 224.0 %all-gather.3.cloned.1.call-start = ((), (), s32[]{:S(2)}) async-start(), calls=%async_computation.4 | async-start | bytes 8847360 | tf_op jit(solution)/shard_map/all_gather | solution.py:60
  50.2 1.2 copy-start
  206.3 5.4 %copy-start.1 = (bf16[8,1,4,36,768]{4,0,3,2,1:T(8,128)(2,1)S(1)}, bf16[8,1,4,36,768]{4,0,3,2,1:T(8,128)(2,1)}, u32[]{:S(2)}) copy-start(bf16[8,1,4,36,768]{4,0,3,2,1:T(8,128)(2,1)} %copy-done) | copy-start | bytes 5308420
  206.3 62.2 %all-to-all-start.2 = ((bf16[4,8,144,1,512]{4,2,1,3,0:T(8,128)(2,1)}), bf16[4,8,144,1,512]{4,2,1,3,0:T(8,128)(2,1)}, u32[]{:S(2)}, u32[]{:S(2)}) async-start(bf16[4,8,144,1,512]{4,2,1,3,0:T(8,128)(2,1)} %pad_maximum_fusion), calls=%async_computation.2 | async-start | bytes 9437184 | tf_op jit(solution)/shard_map/all_to_all | solution.py:12
  268.5 34.0 %all-to-all-start.3 = ((f32[4,1,288]{2,1,0:T(1,128)}), f32[4,1,288]{2,1,0:T(1,128)S(1)}, u32[]{:S(2)}, u32[]{:S(2)}) async-start(f32[4,1,288]{2,1,0:T(1,128)} %all_to_all.25), calls=%async_computation.3 | async-start | bytes 12288 | tf_op jit(solution)/shard_map/all_to_all | solution.py:72
Sparse Core Ops, SparseCore 0:
  9.6 157.4 all-gather.4
  168.7 53.9 all-gather.2
